TPU v7x, 32 devices: a whole 2x2x4 slice. The times are simulated.
32 devices in a mesh: seq: 8 (over z, y), fsdp: 4 (over x, core).
Axes of the slice: x: 2, y: 2, z: 4, core: 2. Of those that a mesh axis runs over, the one named last changes fastest.
Arguments:
- tokens: bfloat16 [2048, 2048], P('seq', 'fsdp'), may hold values from -6 to 6
- deal_order: int32 [8, 8], replicated, may hold values from 0 to 7, each once within a row
- lengths: int32 [4], replicated, may hold values from 1 to 1024, 2048 in all
- x_weight: bfloat16 [2048, 1536], P(None, 'fsdp'), may hold values from -0.0390625 to 0.0390625
- z_weight: bfloat16 [2048, 1536], P(None, 'fsdp'), may hold values from -0.125 to 0.125
- shared_weight: bfloat16 [2048, 512], P('fsdp'), may hold values from -0.0390625 to 0.0390625
- step_weight: bfloat16 [2048, 24], P(None, 'fsdp'), may hold values from -0.125 to 0.125
- conv_heads: float32 [4, 1536], P(None, 'fsdp'), may hold values from -3 to 3
- conv_shared: float32 [4, 512], replicated, may hold values from -3 to 3
- step_bias: float32 [24], P('fsdp'), as said below
- decay_log: float32 [24], P('fsdp'), may hold values from -7.1 to -2.8, as said below
- skip_gain: float32 [24], P('fsdp'), may hold values from 0.5 to 1.5
Outputs:
- mixed: bfloat16 [2048, 1536], P('seq', 'fsdp')
Inputs may be any that keep to these rules, and one draw needn't show every extreme that they name: `deal_order`: each row is a permutation of 0 to 7. The lengths sum to 2048. `decay_log`: one value a head. `step_bias`: one value a head.
All inputs are finite; a program needn't handle non-finite values.
Results may differ from a plain program's by a relative error of at most 0.0095.
Values may be sent and summed in bfloat16 or wider, within the bound.
No kernel may reach another device: no remote copies, remote signals or barrier semaphores. Data moves between devices by JAX's collectives and lax.ppermute only.
A program may use at most 128 MiB of HBM per device.

v0:
```python
import jax
import jax.numpy as jnp
from jax import lax
from jax.sharding import PartitionSpec as P

precise = lax.Precision.HIGHEST


def shifted(array, axis, by):
    count = lax.axis_size(axis)
    pairs = [(i, i + by) for i in range(count) if 0 <= i + by < count]
    return lax.ppermute(array, axis, pairs)


def combine_packed(earlier, later):
    rows = later.shape[1] - 1
    d_e, d_l = (earlier[:, rows:, :], later[:, rows:, :])
    return jnp.concatenate([d_l * earlier[:, :rows, :] + later[:, :rows, :], d_e * d_l], axis=1)


def received(packed, axis, by):
    place = lax.axis_index(axis)
    got = shifted(packed, axis, by)
    rows = packed.shape[1] - 1
    missing = (place < by).astype(packed.dtype)
    return got.at[:, rows:, :].add(missing)


def exclusive_scan(packed, axis):
    count = lax.axis_size(axis)
    if count == 1:
        return received(packed, axis, 1)
    held = received(packed, axis, 1)
    if count > 2:
        held = combine_packed(received(packed, axis, 2), held)
    cover = 2
    while cover < count - 1:
        held = combine_packed(received(held, axis, cover), held)
        cover *= 2
    return held


def segment_of(positions, lengths):
    prompt_ends = jnp.cumsum(lengths)
    counted = (positions[:, None] >= prompt_ends[None, :]).astype(jnp.int32)
    return jnp.sum(counted, axis=1)


def causal_conv(extended, segment_ids, weights, conv_width):
    out_rows = extended.shape[0] - conv_width + 1
    target = segment_ids[conv_width - 1 :]
    running = jnp.zeros((out_rows, extended.shape[1]), jnp.float32)
    for tap_index in range(conv_width):
        matched = (segment_ids[tap_index : tap_index + out_rows] == target).astype(jnp.float32)
        running = (
            running
            + weights[tap_index][None, :]
            * extended[tap_index : tap_index + out_rows]
            * matched[:, None]
        )
    return running


def local_terms(x_heads, b_rows, c_rows, step_size, decay_log, segment_ids, seg_before):
    log_decay = -jnp.exp(decay_log)[None, :] * step_size
    cum_decay = jnp.cumsum(log_decay, axis=0)
    positions_in = jnp.arange(x_heads.shape[0], dtype=jnp.int32)
    same_prompt = (segment_ids[:, None] == segment_ids[None, :]) & (
        positions_in[:, None] >= positions_in[None, :]
    )
    decay_gap = cum_decay.T[:, :, None] - cum_decay.T[:, None, :]
    decay_matrix = jnp.exp(jnp.where(same_prompt[None], decay_gap, -jnp.inf))
    scores = jnp.dot(c_rows, b_rows.T, precision=precise)
    x_step = x_heads * step_size[:, :, None]
    intra = jnp.einsum("hts,shp->thp", scores[None] * decay_matrix, x_step, precision=precise)
    to_end = jnp.exp(
        jnp.where(
            (segment_ids == segment_ids[-1])[:, None], cum_decay[-1][None, :] - cum_decay, -jnp.inf
        )
    )
    state_out = jnp.einsum("shp,sn->hpn", x_step * to_end[:, :, None], b_rows, precision=precise)
    carried = segment_ids == seg_before
    carry_in = jnp.exp(jnp.where(carried[:, None], cum_decay, -jnp.inf))
    block_decay = jnp.where(carried[-1], jnp.exp(cum_decay[-1]), 0.0)
    return (intra, state_out, carry_in, block_decay)


def per_device(
    tokens,
    deal_order,
    lengths,
    x_weight,
    z_weight,
    shared_weight,
    step_weight,
    conv_heads,
    conv_shared,
    step_bias,
    decay_log,
    skip_gain,
):
    seq_count = lax.axis_size("seq")
    own_index = lax.axis_index("seq")
    tok_dev = tokens.shape[0]
    piece_rows = tok_dev // seq_count
    slot_rows = tokens.reshape(seq_count, piece_rows, tokens.shape[1])
    arrived = lax.all_to_all(slot_rows, "seq", split_axis=0, concat_axis=0, tiled=True)
    dealt_row = lax.dynamic_slice_in_dim(deal_order, own_index, 1, 0)[0]
    inverse = jnp.argsort(dealt_row)
    stream_block = jnp.take(arrived, inverse, axis=0).reshape(tok_dev, tokens.shape[1])
    inner_dev = x_weight.shape[1]
    heads_dev = step_weight.shape[1]
    head_dim = inner_dev // heads_dev
    state_dim = shared_weight.shape[1] // 2
    w_full = lax.all_gather(shared_weight, "fsdp", axis=0, tiled=True)
    weight_list = (x_weight, z_weight, step_weight, w_full)
    feature_part = lax.all_gather(stream_block, "fsdp", axis=1, tiled=True)
    x_acc, z_acc, step_acc, bc_acc = tuple(
        (
            jnp.dot(feature_part, weight, preferred_element_type=jnp.float32)
            for weight in weight_list
        )
    )
    x_raw = x_acc.astype(jnp.bfloat16)
    z_raw = z_acc.astype(jnp.bfloat16)
    bc_raw = bc_acc.astype(jnp.bfloat16)
    step_size = jax.nn.softplus(step_acc + step_bias[None, :])
    mixed_in = jnp.concatenate([x_raw, bc_raw], axis=1)
    conv_width = conv_heads.shape[0]
    prior_rows = shifted(mixed_in[tok_dev - conv_width + 1 :], "seq", 1)
    first_pos = own_index * tok_dev
    positions = first_pos - (conv_width - 1) + jnp.arange(tok_dev + conv_width - 1, dtype=jnp.int32)
    seg_ext = segment_of(positions, lengths)
    extended = jnp.concatenate([prior_rows, mixed_in], axis=0).astype(jnp.float32)
    activated = jax.nn.silu(
        causal_conv(
            extended, seg_ext, jnp.concatenate([conv_heads, conv_shared], axis=1), conv_width
        )
    )
    segment_ids = seg_ext[conv_width - 1 :]
    seg_before = jnp.where(own_index == 0, -1, seg_ext[conv_width - 2])
    x_heads = activated[:, :inner_dev].reshape(tok_dev, heads_dev, head_dim)
    b_rows = activated[:, inner_dev : inner_dev + state_dim]
    c_rows = activated[:, inner_dev + state_dim :]
    intra, state_out, carry_in, block_decay = local_terms(
        x_heads, b_rows, c_rows, step_size, decay_log, segment_ids, seg_before
    )
    packed = jnp.concatenate(
        [state_out, jnp.broadcast_to(block_decay[:, None, None], (heads_dev, 1, state_dim))], axis=1
    )
    state_in = exclusive_scan(packed, "seq")[:, :head_dim, :]
    incoming = jnp.einsum("tn,hpn->thp", c_rows, state_in, precision=precise)
    y_block = intra + carry_in[:, :, None] * incoming + skip_gain[None, :, None] * x_heads
    gated = (y_block.reshape(tok_dev, inner_dev) * jax.nn.silu(z_raw.astype(jnp.float32))).astype(
        jnp.bfloat16
    )
    ordered = gated.reshape(seq_count, piece_rows, inner_dev)
    outgoing = jnp.take(ordered, dealt_row, axis=0)
    returned = lax.all_to_all(outgoing, "seq", split_axis=0, concat_axis=0, tiled=True)
    return returned.reshape(tok_dev, inner_dev)


def solution(mesh):
    return jax.shard_map(
        per_device,
        mesh=mesh,
        in_specs=(
            P("seq", "fsdp"),
            P(),
            P(),
            P(None, "fsdp"),
            P(None, "fsdp"),
            P("fsdp", None),
            P(None, "fsdp"),
            P(None, "fsdp"),
            P(),
            P("fsdp"),
            P("fsdp"),
            P("fsdp"),
        ),
        out_specs=P("seq", "fsdp"),
        check_vma=False,
    )
```

profile of v0, /device:TPU:0, one launch (start us, length us, event | category | flops | bytes accessed | tf_op | source)
XLA Modules:
  0.0 161.2 jit_solution(1924981026122222076)
XLA Ops:
  6.6 7.4 %all-to-all-start = ((bf16[8,32,512]{2,1,0:T(8,128)(2,1)}), bf16[8,32,512]{2,1,0:T(8,128)(2,1)S(1)}, u32[]{:S(2)}, u32[]{:S(2)}) async-start(bf16[8,32,512]{2,1,0:T(8,128)(2,1)} %bitcast.85), calls=%async_computation | async-start | bytes 524288 | tf_op jit(solution)/shard_map/all_to_all | solution.py:107
  14.0 1.3 compare_and_fusion.1
  15.3 1.0 sort.17
  16.5 6.4 %all-to-all-done = bf16[8,32,512]{2,1,0:T(8,128)(2,1)S(1)} async-done(((bf16[8,32,512]{2,1,0:T(8,128)(2,1)}), bf16[8,32,512]{2,1,0:T(8,128)(2,1)S(1)}, u32[]{:S(2)}, u32[]{:S(2)}) %all-to-all-start) | async-done | bytes 262176 | tf_op jit(solution)/shard_map/all_to_all | solution.py:107
  23.5 0.8 bitcast_select_fusion
  26.5 1.3 broadcast_compare_fusion
  29.2 11.1 %all-gather.3.cloned.1.call-done = bf16[256,2048]{1,0:T(8,128)(2,1)} async-done(((bf16[256,512]{1,0:T(8,128)(2,1)}), bf16[256,2048]{1,0:T(8,128)(2,1)}) %all-gather.3.cloned.1.call-update) | async-done | bytes 1048592 | tf_op jit(solution)/shard_map/all_gather | solution.py:117
  40.2 1.6 %fusion.41 = (f32[6,256]{1,0:T(8,128)S(1)}, f32[256,6]{0,1:T(8,128)S(1)}) fusion(f32[6]{0:T(128)S(1)} %exponential_negate_fusion, f32[6]{0:T(128)S(1)} %copy-done.19, bf16[256,2048]{1,0:T(8,128)(2,1)} %all-gather.3.cloned.1.call-done, bf16[2048,6]{0,1:T(8,128)(2,1)S(1)} %copy-done.4), kind=kOutput, calls=%fused_computation.64 | convolution fusion | flops 6303744 | bytes 1085488 | tf_op jit(solution)/shard_map/dot_general | solution.py:120
  41.9 1.8 %reduce-window.19 = f32[6,2,128]{2,1,0:T(2,128)S(1)} reduce-window(f32[6,2,128]{2,1,0:T(2,128)S(1)} %reshape.288, f32[]{:T(128)} %constant.149.clone.1), window={size=1x1x128 pad=0_0x0_0x127_0}, to_apply=%region_3.4 | reduce-window | flops 195072 | bytes 12292 | tf_op jit(solution)/shard_map/reduce-window.1
  45.4 1.9 %convolution_convert_fusion.2 = bf16[256,384]{1,0:T(8,128)(2,1)S(1)} fusion(bf16[256,2048]{1,0:T(8,128)(2,1)} %all-gather.3.cloned.1.call-done, bf16[2048,384]{1,0:T(8,128)(2,1)S(1)} %copy-done), kind=kOutput, calls=%fused_computation.14 | convolution fusion | flops 402751488 | bytes 2818048 | tf_op jit(solution)/shard_map/dot_general | solution.py:120
  47.3 17.1 %all-gather.5.cloned.1.call-done = bf16[2048,512]{1,0:T(8,128)(2,1)} async-done(((bf16[512,512]{1,0:T(8,128)(2,1)}), bf16[2048,512]{1,0:T(8,128)(2,1)}) %all-gather.5.cloned.1.call-update) | async-done | bytes 2097168 | tf_op jit(solution)/shard_map/all_gather | solution.py:115
  64.4 2.3 %convolution_convert_fusion = bf16[256,512]{1,0:T(8,128)(2,1)S(1)} fusion(bf16[256,2048]{1,0:T(8,128)(2,1)S(1)} %copy-done.1, bf16[2048,512]{1,0:T(8,128)(2,1)} %all-gather.5.cloned.1.call-done), kind=kOutput, calls=%fused_computation.8 | convolution fusion | flops 537001984 | bytes 3407872 | tf_op jit(solution)/shard_map/dot_general | solution.py:120
  66.8 3.4 %collective-permute-start = (bf16[3,896]{1,0:T(4,128)(2,1)S(1)}, bf16[3,896]{1,0:T(4,128)(2,1)S(1)}, u32[]{:S(2)}, u32[]{:S(2)}) collective-permute-start(bf16[3,896]{1,0:T(4,128)(2,1)S(1)} %pad_maximum_fusion.3), channel_id=1, source_target_pairs={{0,4},{4,8},{8,12},{12,16},{16,20},{20,24},{24,28},{1,5},{5,9},{9,... | collective-permute-start | bytes 16136 | tf_op jit(solution)/shard_map/ppermute | solution.py:12
  70.2 1.2 broadcast_select_fusion.1
  73.1 1.9 %copy.39 = f32[256,384]{0,1:T(8,128)} copy(f32[256,384]{1,0:T(8,128)} %slice.219) | data formatting | bytes 786432 | tf_op jit(solution)/shard_map/slice | solution.py:142
  75.1 1.5 fusion.25
  78.1 5.9 %collective-permute-start.2 = (f32[6,65,256]{2,1,0:T(8,128)}, f32[6,65,256]{2,1,0:T(8,128)}, u32[]{:S(2)}, u32[]{:S(2)}) collective-permute-start(f32[6,65,256]{2,1,0:T(8,128)} %pad_maximum_fusion), channel_id=1, source_target_pairs={{0,8},{4,12},{8,16},{12,20},{16,24},{20,28},{1,9},{5,13},{9,17},{1... | collective-permute-start | bytes 1198088 | tf_op jit(solution)/shard_map/ppermute | solution.py:12
  83.9 3.2 %collective-permute-start.1 = (f32[6,65,256]{2,1,0:T(8,128)}, f32[6,65,256]{2,1,0:T(8,128)}, u32[]{:S(2)}, u32[]{:S(2)}) collective-permute-start(f32[6,65,256]{2,1,0:T(8,128)} %pad_maximum_fusion), channel_id=1, source_target_pairs={{0,4},{4,8},{8,12},{12,16},{16,20},{20,24},{24,28},{1,5},{5,9},{9,... | collective-permute-start | bytes 1198088 | tf_op jit(solution)/shard_map/ppermute | solution.py:12
  87.8 0.8 fusion.49
  88.7 0.9 fusion.31
  89.5 2.6 %collective-permute-done.2 = f32[6,65,256]{2,1,0:T(8,128)} collective-permute-done((f32[6,65,256]{2,1,0:T(8,128)}, f32[6,65,256]{2,1,0:T(8,128)}, u32[]{:S(2)}, u32[]{:S(2)}) %collective-permute-start.2) | collective-permute-done | bytes 399392 | tf_op jit(solution)/shard_map/ppermute | solution.py:12
  92.1 3.0 %collective-permute-done.1 = f32[6,65,256]{2,1,0:T(8,128)} collective-permute-done((f32[6,65,256]{2,1,0:T(8,128)}, f32[6,65,256]{2,1,0:T(8,128)}, u32[]{:S(2)}, u32[]{:S(2)}) %collective-permute-start.1) | collective-permute-done | bytes 399392 | tf_op jit(solution)/shard_map/ppermute | solution.py:12
  95.1 0.8 fusion.47
  96.0 1.2 slice_add_fusion
  97.2 10.9 %collective-permute-start.3 = (f32[6,65,256]{2,1,0:T(8,128)S(1)}, f32[6,65,256]{2,1,0:T(8,128)S(1)}, u32[]{:S(2)}, u32[]{:S(2)}) collective-permute-start(f32[6,65,256]{2,1,0:T(8,128)S(1)} %pad_maximum_fusion.1), channel_id=1, source_target_pairs={{0,8},{4,12},{8,16},{12,20},{16,24},{20,28},{1,9},{5,13},{9,17},{1... | collective-permute-start | bytes 1198088 | tf_op jit(solution)/shard_map/ppermute | solution.py:12
  108.7 1.4 fusion.10
  110.2 5.7 %collective-permute-done.3 = f32[6,65,256]{2,1,0:T(8,128)S(1)} collective-permute-done((f32[6,65,256]{2,1,0:T(8,128)S(1)}, f32[6,65,256]{2,1,0:T(8,128)S(1)}, u32[]{:S(2)}, u32[]{:S(2)}) %collective-permute-start.3) | collective-permute-done | bytes 399392 | tf_op jit(solution)/shard_map/ppermute | solution.py:12
  116.0 5.3 %collective-permute-start.4 = (f32[6,65,256]{2,1,0:T(8,128)S(1)}, f32[6,65,256]{2,1,0:T(8,128)S(1)}, u32[]{:S(2)}, u32[]{:S(2)}) collective-permute-start(f32[6,65,256]{2,1,0:T(8,128)S(1)} %pad_maximum_fusion.2), channel_id=1, source_target_pairs={{0,16},{4,20},{8,24},{12,28},{1,17},{5,21},{9,25},{13,29},{2,18},{... | collective-permute-start | bytes 1198088 | tf_op jit(solution)/shard_map/ppermute | solution.py:12
  121.7 1.9 %fusion.5 = f32[256,6,64]{0,2,1:T(8,128)S(1)} fusion(f32[6,256]{1,0:T(8,128)S(1)} %bitcast.90, f32[256,256]{1,0:T(8,128)S(1)} %fusion.33, pred[256,256]{1,0:T(8,128)(4,1)S(1)} %fusion.31, f32[256,6,64]{0,2,1:T(8,128)S(1)} %bitcast.80, f32[256,6]{0,1:T(8,128)S(1)} %get-tuple-element.76), kind=kOutput, calls=%fused_computation.7 | convolution fusion | flops 303267840 | bytes 1126400 | tf_op jit(solution)/shard_map/hts,shp->thp/dot_general | solution.py:75
  123.6 4.5 %collective-permute-done.4 = f32[6,65,256]{2,1,0:T(8,128)S(1)} collective-permute-done((f32[6,65,256]{2,1,0:T(8,128)S(1)}, f32[6,65,256]{2,1,0:T(8,128)S(1)}, u32[]{:S(2)}, u32[]{:S(2)}) %collective-permute-start.4) | collective-permute-done | bytes 399392 | tf_op jit(solution)/shard_map/ppermute | solution.py:12
  128.8 1.1 multiply_convert_fusion
  130.8 22.9 %all_to_all.10 = bf16[8,32,384]{2,1,0:T(8,128)(2,1)S(1)} all-to-all(bf16[8,32,384]{2,1,0:T(8,128)(2,1)S(1)} %broadcast_select_fusion), channel_id=1, replica_groups=mesh['seq'=8,'fsdp'=4] {'seq'}, dimensions={0} | all-to-all | bytes 393216 | tf_op jit(solution)/shard_map/all_to_all | solution.py:159
  (98 shorter events, 12.6 us)
Async XLA Ops:
  6.5 38.8 %copy-start = (bf16[2048,384]{1,0:T(8,128)(2,1)S(1)}, bf16[2048,384]{1,0:T(8,128)(2,1)}, u32[]{:S(2)}) copy-start(bf16[2048,384]{1,0:T(8,128)(2,1)} %param.23) | copy-start | bytes 4718596
  6.5 18.5 %copy-start.21 = (s32[4]{0:T(128)S(1)}, s32[4]{0:T(128)}, u32[]{:S(2)}) copy-start(s32[4]{0:T(128)} %param.22) | copy-start | bytes 52
  6.5 22.0 %copy-start.14 = (f32[4,384]{1,0:T(4,128)S(1)}, f32[4,384]{1,0:T(4,128)}, u32[]{:S(2)}) copy-start(f32[4,384]{1,0:T(4,128)} %param.27) | copy-start | bytes 18436
  6.5 22.0 %copy-start.13 = (f32[4,512]{1,0:T(4,128)S(1)}, f32[4,512]{1,0:T(4,128)}, u32[]{:S(2)}) copy-start(f32[4,512]{1,0:T(4,128)} %param.28) | copy-start | bytes 24580
  6.5 22.6 %copy-start.22 = (f32[6]{0:T(128)S(1)}, f32[6]{0:T(128)}, u32[]{:S(2)}) copy-start(f32[6]{0:T(128)} %param.30) | copy-start | bytes 76
  6.5 33.7 %copy-start.19 = (f32[6]{0:T(128)S(1)}, f32[6]{0:T(128)}, u32[]{:S(2)}) copy-start(f32[6]{0:T(128)} %param.29) | copy-start | bytes 76
  6.6 33.7 %copy-start.4 = (bf16[2048,6]{0,1:T(8,128)(2,1)S(1)}, bf16[2048,6]{0,1:T(8,128)(2,1)}, u32[]{:S(2)}) copy-start(bf16[2048,6]{0,1:T(8,128)(2,1)} %param.26) | copy-start | bytes 73732
  6.6 16.3 %all-to-all-start = ((bf16[8,32,512]{2,1,0:T(8,128)(2,1)}), bf16[8,32,512]{2,1,0:T(8,128)(2,1)S(1)}, u32[]{:S(2)}, u32[]{:S(2)}) async-start(bf16[8,32,512]{2,1,0:T(8,128)(2,1)} %bitcast.85), calls=%async_computation | async-start | bytes 524288 | tf_op jit(solution)/shard_map/all_to_all | solution.py:107
  14.0 26.2 %all-gather.3.cloned.1.call-start = ((), (), s32[]{:S(2)}) async-start(), calls=%async_computation.2 | async-start | bytes 1310720 | tf_op jit(solution)/shard_map/all_gather | solution.py:117
  24.3 40.1 %all-gather.5.cloned.1.call-start = ((), (), s32[]{:S(2)}) async-start(), calls=%async_computation.3 | async-start | bytes 2621440 | tf_op jit(solution)/shard_map/all_gather | solution.py:115
  25.4 14.9 %copy-start.5 = (s32[259]{0:T(512)}, s32[259]{0:T(512)S(1)}, u32[]{:S(2)}) copy-start(s32[259]{0:T(512)S(1)} %convert_reduce_fusion) | copy-start | bytes 3112
  41.9 22.5 %copy-start.1 = (bf16[256,2048]{1,0:T(8,128)(2,1)S(1)}, bf16[256,2048]{1,0:T(8,128)(2,1)}, u32[]{:S(2)}) copy-start(bf16[256,2048]{1,0:T(8,128)(2,1)} %all-gather.3.cloned.1.call-done) | copy-start | bytes 3145732
  44.1 0.6 copy-start.7
  66.7 4.9 %copy-start.9 = (f32[896]{0:T(1024)S(1)}, f32[896]{0:T(1024)}, u32[]{:S(2)}) copy-start(f32[896]{0:T(1024)} %get-tuple-element.55) | copy-start | bytes 10756
  66.7 4.9 %copy-start.10 = (f32[896]{0:T(1024)S(1)}, f32[896]{0:T(1024)}, u32[]{:S(2)}) copy-start(f32[896]{0:T(1024)} %get-tuple-element.56) | copy-start | bytes 10756
  66.7 4.9 %copy-start.11 = (f32[896]{0:T(1024)S(1)}, f32[896]{0:T(1024)}, u32[]{:S(2)}) copy-start(f32[896]{0:T(1024)} %get-tuple-element.57) | copy-start | bytes 10756
  66.7 4.9 %copy-start.12 = (f32[896]{0:T(1024)S(1)}, f32[896]{0:T(1024)}, u32[]{:S(2)}) copy-start(f32[896]{0:T(1024)} %get-tuple-element.58) | copy-start | bytes 10756
  66.7 4.9 %copy-start.15 = (f32[256]{0:T(256)S(1)}, f32[256]{0:T(256)}, u32[]{:S(2)}) copy-start(f32[256]{0:T(256)} %get-tuple-element.69) | copy-start | bytes 3076
  66.8 4.9 %copy-start.16 = (f32[256]{0:T(256)S(1)}, f32[256]{0:T(256)}, u32[]{:S(2)}) copy-start(f32[256]{0:T(256)} %get-tuple-element.70) | copy-start | bytes 3076
  66.8 4.9 %copy-start.17 = (f32[256]{0:T(256)S(1)}, f32[256]{0:T(256)}, u32[]{:S(2)}) copy-start(f32[256]{0:T(256)} %get-tuple-element.71) | copy-start | bytes 3076
  66.8 4.7 %collective-permute-start = (bf16[3,896]{1,0:T(4,128)(2,1)S(1)}, bf16[3,896]{1,0:T(4,128)(2,1)S(1)}, u32[]{:S(2)}, u32[]{:S(2)}) collective-permute-start(bf16[3,896]{1,0:T(4,128)(2,1)S(1)} %pad_maximum_fusion.3), channel_id=1, source_target_pairs={{0,4},{4,8},{8,12},{12,16},{16,20},{20,24},{24,28},{1,5},{5,9},{9,... | collective-permute-start | bytes 16136 | tf_op jit(solution)/shard_map/ppermute | solution.py:12
  75.0 12.1 %copy-start.6 = (s32[259]{0:T(512)S(1)}, s32[259]{0:T(512)}, u32[]{:S(2)}) copy-start(s32[259]{0:T(512)} %copy-done.5) | copy-start | bytes 3112
  78.1 14.1 %collective-permute-start.2 = (f32[6,65,256]{2,1,0:T(8,128)}, f32[6,65,256]{2,1,0:T(8,128)}, u32[]{:S(2)}, u32[]{:S(2)}) collective-permute-start(f32[6,65,256]{2,1,0:T(8,128)} %pad_maximum_fusion), channel_id=1, source_target_pairs={{0,8},{4,12},{8,16},{12,20},{16,24},{20,28},{1,9},{5,13},{9,17},{1... | collective-permute-start | bytes 1198088 | tf_op jit(solution)/shard_map/ppermute | solution.py:12
  83.9 11.2 %collective-permute-start.1 = (f32[6,65,256]{2,1,0:T(8,128)}, f32[6,65,256]{2,1,0:T(8,128)}, u32[]{:S(2)}, u32[]{:S(2)}) collective-permute-start(f32[6,65,256]{2,1,0:T(8,128)} %pad_maximum_fusion), channel_id=1, source_target_pairs={{0,4},{4,8},{8,12},{12,16},{16,20},{20,24},{24,28},{1,5},{5,9},{9,... | collective-permute-start | bytes 1198088 | tf_op jit(solution)/shard_map/ppermute | solution.py:12
  87.8 20.9 %copy-start.3 = (bf16[2048,384]{1,0:T(8,128)(2,1)S(1)}, bf16[2048,384]{1,0:T(8,128)(2,1)}, u32[]{:S(2)}) copy-start(bf16[2048,384]{1,0:T(8,128)(2,1)} %param.24) | copy-start | bytes 4718596
  97.2 18.7 %collective-permute-start.3 = (f32[6,65,256]{2,1,0:T(8,128)S(1)}, f32[6,65,256]{2,1,0:T(8,128)S(1)}, u32[]{:S(2)}, u32[]{:S(2)}) collective-permute-start(f32[6,65,256]{2,1,0:T(8,128)S(1)} %pad_maximum_fusion.1), channel_id=1, source_target_pairs={{0,8},{4,12},{8,16},{12,20},{16,24},{20,28},{1,9},{5,13},{9,17},{1... | collective-permute-start | bytes 1198088 | tf_op jit(solution)/shard_map/ppermute | solution.py:12
  110.2 11.6 %copy-start.2 = (f32[256,384]{0,1:T(8,128)S(1)}, f32[256,384]{0,1:T(8,128)}, u32[]{:S(2)}) copy-start(f32[256,384]{0,1:T(8,128)} %copy.39) | copy-start | bytes 1179652
  110.2 11.6 %copy-start.8 = (f32[1,6,2,128]{3,1,2,0:T(8,128)S(1)}, f32[1,6,2,128]{3,1,2,0:T(8,128)}, u32[]{:S(2)}) copy-start(f32[1,6,2,128]{3,1,2,0:T(8,128)} %copy-done.7) | copy-start | bytes 18436
  115.9 12.2 %copy-start.20 = (f32[6]{0:T(128)S(1)}, f32[6]{0:T(128)}, u32[]{:S(2)}) copy-start(f32[6]{0:T(128)} %param.31) | copy-start | bytes 76
  116.0 12.2 %collective-permute-start.4 = (f32[6,65,256]{2,1,0:T(8,128)S(1)}, f32[6,65,256]{2,1,0:T(8,128)S(1)}, u32[]{:S(2)}, u32[]{:S(2)}) collective-permute-start(f32[6,65,256]{2,1,0:T(8,128)S(1)} %pad_maximum_fusion.2), channel_id=1, source_target_pairs={{0,16},{4,20},{8,24},{12,28},{1,17},{5,21},{9,25},{13,29},{2,18},{... | collective-permute-start | bytes 1198088 | tf_op jit(solution)/shard_map/ppermute | solution.py:12
  128.7 2.0 %copy-start.18 = (pred[8]{0:T(512)(128)(4,1)S(1)}, pred[8]{0:T(512)(128)(4,1)}, u32[]{:S(2)}) copy-start(pred[8]{0:T(512)(128)(4,1)} %get-tuple-element.59) | copy-start | bytes 28
Sparse Core Ops, SparseCore 0:
  24.4 15.7 all-gather.2
  41.8 22.5 all-gather.4
where the time goes:
time: 162 us; the launch traced here: 161 us
  waiting for transfers between devices  51.2 us (32%)
  starting transfers between devices  36.3 us (22%)
  blocking collectives  22.9 us (14%)
  other arithmetic  15.7 us (10%)
  between operations  14.4 us (9%)
  matrix products  11.6 us (7%)
  local copies, waits for them, and re-layouts  9.22 us (6%)
    ppermute x5, starting transfers between devices, shifted(): return lax.ppermute(array, axis, pairs)  28.8 us
    all_to_all x1, blocking collectives, per_device(): lax.all_to_all(outgoing, 'seq', split_axis=0, concat_axis=0, tiled=True)  22.9 us
    all_gather x1, waiting for transfers between devices, per_device(): w_full = lax.all_gather(shared_weight, 'fsdp', axis=0, tiled=True)  17.1 us
    ppermute x5, waiting for transfers between devices, shifted(): return lax.ppermute(array, axis, pairs)  15.9 us
    all_gather x1, waiting for transfers between devices, per_device(): feature_part = lax.all_gather(stream_block, 'fsdp', axis=1, tiled=True)  11.1 us
    all_to_all x1, starting transfers between devices, per_device(): lax.all_to_all(slot_rows, 'seq', split_axis=0, concat_axis=0, tiled=True)  7.42 us
    dot_general x4, matrix products, per_device(): jnp.dot(feature_part, weight, preferred_element_type=jnp.float32)  7.29 us
    all_to_all x1, waiting for transfers between devices, per_device(): lax.all_to_all(slot_rows, 'seq', split_axis=0, concat_axis=0, tiled=True)  6.42 us
  transfers between devices with their start and end apart: 8, of which 8 were waited for; matrix products, arithmetic and copies ran while one was open for 13% of the time, Pallas kernels for 0%

commit v1 on v0

--- a/solution.py
+++ b/solution.py
@@ -99,6 +99,23 @@
     decay_log,
     skip_gain,
 ):
+
+    def define_words_on_mesh(inner_x):
+        axis_name = "fsdp"
+        nd = lax.axis_size(axis_name)
+        local_next = [(nth - 1, nth) for nth in range(1, nd)] + [(nd - 1, 0)]
+        b_next = inner_x
+        line_up = [b_next]
+        b = 0
+        while b < nd - 1:
+            b_next = lax.ppermute(b_next, axis_name, local_next)
+            line_up += [b_next]
+            b += 1
+        far_arr = jnp.concatenate([*reversed(line_up)], axis=1)
+        kept_arr = lax.axis_index(axis_name)
+        step_out = jnp.roll(far_arr, (kept_arr + 1) * b_next.shape[1], axis=1)
+        return step_out
+
     seq_count = lax.axis_size("seq")
     own_index = lax.axis_index("seq")
     tok_dev = tokens.shape[0]
@@ -114,7 +131,7 @@
     state_dim = shared_weight.shape[1] // 2
     w_full = lax.all_gather(shared_weight, "fsdp", axis=0, tiled=True)
     weight_list = (x_weight, z_weight, step_weight, w_full)
-    feature_part = lax.all_gather(stream_block, "fsdp", axis=1, tiled=True)
+    feature_part = define_words_on_mesh(stream_block)
     x_acc, z_acc, step_acc, bc_acc = tuple(
         (
             jnp.dot(feature_part, weight, preferred_element_type=jnp.float32)

time: 162 us -> 149 us (0.920)
  blocking collectives: 22.9 us -> 33.2 us
  waiting for transfers between devices: 51.2 us -> 41.7 us
  other arithmetic: 15.7 us -> 9.43 us
  starting transfers between devices: 36.3 us -> 30.5 us
  local copies, waits for them, and re-layouts: 9.22 us -> 7.54 us
    ppermute x0 -> x3, waiting for transfers between devices: none -> 21.6 us  [define_words_on_mesh(): b_next = lax.ppermute(b_next, axis_name, local_next)]
    all_gather x1, waiting for transfers between devices: 17.1 us -> 0.02 us  [per_device(): w_full = lax.all_gather(shared_weight, 'fsdp', axis=0, tiled=True)]
    all_gather x1 -> x0, waiting for transfers between devices: 11.1 us -> none  [per_device(): feature_part = lax.all_gather(stream_block, 'fsdp', axis=1, tiled=True)]
    all_to_all x1, blocking collectives: 22.9 us -> 33.2 us  [per_device(): lax.all_to_all(outgoing, 'seq', split_axis=0, concat_axis=0, tiled=True)]
    ppermute x5, starting transfers between devices: 28.8 us -> 21.9 us  [shifted(): return lax.ppermute(array, axis, pairs)]
    slice x2, local copies, waits for them, and re-layouts: 2.68 us -> 0.19 us  [per_device(): x_heads = activated[:, :inner_dev].reshape(tok_dev, heads_dev, head_dim)]
    ppermute x5, waiting for transfers between devices: 15.9 us -> 13.8 us  [shifted(): return lax.ppermute(array, axis, pairs)]
    unnamed x52 -> x31, local copies, waits for them, and re-layouts: 1.2 us -> 2.93 us
  transfers between devices with their start and end apart: 8 -> 10, of which waited for: 8 -> 9; matrix products, arithmetic and copies ran while one was open for 13% -> 11% of each run, Pallas kernels for 0% -> 0%
where the time goes in v1:
time: 149 us; the launch traced here: 148 us
  waiting for transfers between devices  41.7 us (28%)
  blocking collectives  33.2 us (22%)
  starting transfers between devices  30.5 us (20%)
  between operations  14.5 us (10%)
  matrix products  11.2 us (8%)
  other arithmetic  9.43 us (6%)
  local copies, waits for them, and re-layouts  7.54 us (5%)
    all_to_all x1, blocking collectives, per_device(): lax.all_to_all(outgoing, 'seq', split_axis=0, concat_axis=0, tiled=True)  33.2 us
    ppermute x5, starting transfers between devices, shifted(): return lax.ppermute(array, axis, pairs)  21.9 us
    ppermute x3, waiting for transfers between devices, define_words_on_mesh(): b_next = lax.ppermute(b_next, axis_name, local_next)  21.6 us
    ppermute x5, waiting for transfers between devices, shifted(): return lax.ppermute(array, axis, pairs)  13.8 us
    all_to_all x1, starting transfers between devices, per_device(): lax.all_to_all(slot_rows, 'seq', split_axis=0, concat_axis=0, tiled=True)  7.42 us
    dot_general x4, matrix products, per_device(): jnp.dot(feature_part, weight, preferred_element_type=jnp.float32)  7.1 us
    all_to_all x1, waiting for transfers between devices, per_device(): lax.all_to_all(slot_rows, 'seq', split_axis=0, concat_axis=0, tiled=True)  5.63 us
  transfers between devices with their start and end apart: 10, of which 9 were waited for; matrix products, arithmetic and copies ran while one was open for 11% of the time, Pallas kernels for 0%

profile of v1, /device:TPU:0, one launch (start us, length us, event | category | flops | bytes accessed | tf_op | source)
XLA Modules:
  0.0 148.0 jit_solution(18145284165127408943)
XLA Ops:
  6.5 7.4 %all-to-all-start = ((bf16[8,32,512]{2,1,0:T(8,128)(2,1)}), bf16[8,32,512]{2,1,0:T(8,128)(2,1)S(1)}, u32[]{:S(2)}, u32[]{:S(2)}) async-start(bf16[8,32,512]{2,1,0:T(8,128)(2,1)} %bitcast.81), calls=%async_computation | async-start | bytes 524288 | tf_op jit(solution)/shard_map/all_to_all | solution.py:124
  14.7 0.7 compare_and_fusion.1
  15.4 1.0 sort.17
  16.6 0.7 constant_dynamic-update-slice_fusion.1
  17.3 5.6 %all-to-all-done = bf16[8,32,512]{2,1,0:T(8,128)(2,1)S(1)} async-done(((bf16[8,32,512]{2,1,0:T(8,128)(2,1)}), bf16[8,32,512]{2,1,0:T(8,128)(2,1)S(1)}, u32[]{:S(2)}, u32[]{:S(2)}) %all-to-all-start) | async-done | bytes 262176 | tf_op jit(solution)/shard_map/all_to_all | solution.py:124
  23.9 9.1 %collective-permute-done = bf16[256,512]{1,0:T(8,128)(2,1)S(1)} collective-permute-done((bf16[256,512]{1,0:T(8,128)(2,1)S(1)}, bf16[256,512]{1,0:T(8,128)(2,1)S(1)}, u32[]{:S(2)}, u32[]{:S(2)}) %collective-permute-start) | collective-permute-done | bytes 262176 | tf_op jit(solution)/shard_map/ppermute | solution.py:111
  33.0 1.0 collective-permute-start.1
  35.4 0.7 broadcast_compare_fusion
  36.1 7.4 %collective-permute-done.1 = bf16[256,512]{1,0:T(8,128)(2,1)S(1)} collective-permute-done((bf16[256,512]{1,0:T(8,128)(2,1)S(1)}, bf16[256,512]{1,0:T(8,128)(2,1)S(1)}, u32[]{:S(2)}, u32[]{:S(2)}) %collective-permute-start.1) | collective-permute-done | bytes 262176 | tf_op jit(solution)/shard_map/ppermute | solution.py:111
  44.1 5.1 %collective-permute-done.2 = bf16[256,512]{1,0:T(8,128)(2,1)S(1)} collective-permute-done((bf16[256,512]{1,0:T(8,128)(2,1)S(1)}, bf16[256,512]{1,0:T(8,128)(2,1)S(1)}, u32[]{:S(2)}, u32[]{:S(2)}) %collective-permute-start.2) | collective-permute-done | bytes 262176 | tf_op jit(solution)/shard_map/ppermute | solution.py:111
  49.5 1.3 copy-done.1
  51.3 1.8 %reduce-window.19 = f32[6,2,128]{2,1,0:T(2,128)S(1)} reduce-window(f32[6,2,128]{2,1,0:T(2,128)S(1)} %reshape.288, f32[]{:T(128)} %constant.176.clone.1), window={size=1x1x128 pad=0_0x0_0x127_0}, to_apply=%region_3.4 | reduce-window | flops 195072 | bytes 12292 | tf_op jit(solution)/shard_map/reduce-window.1
  53.8 1.9 %convolution_convert_fusion.2 = bf16[256,384]{1,0:T(8,128)(2,1)S(1)} fusion(bf16[2048,384]{1,0:T(8,128)(2,1)S(1)} %copy-done, bf16[256,4096]{1,0:T(8,128)(2,1)} %copy-done.1, s32[]{:T(128)S(6)} %select_n.84), kind=kOutput, calls=%fused_computation.14 | convolution fusion | flops 402751488 | bytes 2818052 | tf_op jit(solution)/shard_map/dot_general | solution.py:137
  55.8 2.6 %convolution_convert_fusion = bf16[256,512]{1,0:T(8,128)(2,1)S(1)} fusion(bf16[2048,512]{1,0:T(8,128)(2,1)} %all-gather.2.cloned.1.call-done, bf16[256,4096]{1,0:T(8,128)(2,1)} %copy-done.1, s32[]{:T(128)S(6)} %select_n.84), kind=kOutput, calls=%fused_computation.8 | convolution fusion | flops 537001984 | bytes 3407876 | tf_op jit(solution)/shard_map/dot_general | solution.py:137
  58.4 3.3 %collective-permute-start.3 = (bf16[3,896]{1,0:T(4,128)(2,1)S(1)}, bf16[3,896]{1,0:T(4,128)(2,1)S(1)}, u32[]{:S(2)}, u32[]{:S(2)}) collective-permute-start(bf16[3,896]{1,0:T(4,128)(2,1)S(1)} %pad_maximum_fusion.3), channel_id=1, source_target_pairs={{0,4},{4,8},{8,12},{12,16},{16,20},{20,24},{24,28},{1,5},{5,9},{9,... | collective-permute-start | bytes 16136 | tf_op jit(solution)/shard_map/ppermute | solution.py:12
  63.2 0.7 divide_multiply_fusion
  64.7 5.0 %collective-permute-start.4 = (f32[6,65,256]{2,1,0:T(8,128)S(1)}, f32[6,65,256]{2,1,0:T(8,128)}, u32[]{:S(2)}, u32[]{:S(2)}) collective-permute-start(f32[6,65,256]{2,1,0:T(8,128)S(1)} %pad_maximum_fusion), channel_id=1, source_target_pairs={{0,4},{4,8},{8,12},{12,16},{16,20},{20,24},{24,28},{1,5},{5,9},{9,... | collective-permute-start | bytes 1198088 | tf_op jit(solution)/shard_map/ppermute | solution.py:12
  69.6 2.4 %collective-permute-start.5 = (f32[6,65,256]{2,1,0:T(8,128)S(1)}, f32[6,65,256]{2,1,0:T(8,128)}, u32[]{:S(2)}, u32[]{:S(2)}) collective-permute-start(f32[6,65,256]{2,1,0:T(8,128)S(1)} %pad_maximum_fusion), channel_id=1, source_target_pairs={{0,8},{4,12},{8,16},{12,20},{16,24},{20,28},{1,9},{5,13},{9,17},{1... | collective-permute-start | bytes 1198088 | tf_op jit(solution)/shard_map/ppermute | solution.py:12
  72.3 4.2 %collective-permute-done.4 = f32[6,65,256]{2,1,0:T(8,128)} collective-permute-done((f32[6,65,256]{2,1,0:T(8,128)S(1)}, f32[6,65,256]{2,1,0:T(8,128)}, u32[]{:S(2)}, u32[]{:S(2)}) %collective-permute-start.4) | collective-permute-done | bytes 399392 | tf_op jit(solution)/shard_map/ppermute | solution.py:12
  76.4 2.5 %collective-permute-done.5 = f32[6,65,256]{2,1,0:T(8,128)} collective-permute-done((f32[6,65,256]{2,1,0:T(8,128)S(1)}, f32[6,65,256]{2,1,0:T(8,128)}, u32[]{:S(2)}, u32[]{:S(2)}) %collective-permute-start.5) | collective-permute-done | bytes 399392 | tf_op jit(solution)/shard_map/ppermute | solution.py:12
  78.9 0.8 fusion.51
  79.7 1.2 slice_add_fusion
  81.0 6.5 %collective-permute-start.6 = (f32[6,65,256]{2,1,0:T(8,128)S(1)}, f32[6,65,256]{2,1,0:T(8,128)S(1)}, u32[]{:S(2)}, u32[]{:S(2)}) collective-permute-start(f32[6,65,256]{2,1,0:T(8,128)S(1)} %pad_maximum_fusion.1), channel_id=1, source_target_pairs={{0,8},{4,12},{8,16},{12,20},{16,24},{20,28},{1,9},{5,13},{9,17},{1... | collective-permute-start | bytes 1198088 | tf_op jit(solution)/shard_map/ppermute | solution.py:12
  87.5 0.7 fusion.53
  88.2 2.1 %fusion.10 = f32[256,384]{1,0:T(8,128)S(1)} fusion(bf16[2048,384]{1,0:T(8,128)(2,1)} %param.24, bf16[256,4096]{1,0:T(8,128)(2,1)S(1)} %copy-done.2, s32[]{:T(128)S(6)} %select_n.84), kind=kOutput, calls=%fused_computation.13 | convolution fusion | flops 402849792 | bytes 3014660 | tf_op jit(solution)/shard_map/dot_general | solution.py:137
  90.3 2.9 %collective-permute-done.6 = f32[6,65,256]{2,1,0:T(8,128)S(1)} collective-permute-done((f32[6,65,256]{2,1,0:T(8,128)S(1)}, f32[6,65,256]{2,1,0:T(8,128)S(1)}, u32[]{:S(2)}, u32[]{:S(2)}) %collective-permute-start.6) | collective-permute-done | bytes 399392 | tf_op jit(solution)/shard_map/ppermute | solution.py:12
  93.4 4.7 %collective-permute-start.7 = (f32[6,65,256]{2,1,0:T(8,128)S(1)}, f32[6,65,256]{2,1,0:T(8,128)S(1)}, u32[]{:S(2)}, u32[]{:S(2)}) collective-permute-start(f32[6,65,256]{2,1,0:T(8,128)S(1)} %pad_maximum_fusion.2), channel_id=1, source_target_pairs={{0,16},{4,20},{8,24},{12,28},{1,17},{5,21},{9,25},{13,29},{2,18},{... | collective-permute-start | bytes 1198088 | tf_op jit(solution)/shard_map/ppermute | solution.py:12
  98.5 1.9 %fusion.5 = f32[256,6,64]{0,2,1:T(8,128)S(1)} fusion(f32[6,256]{1,0:T(8,128)S(1)} %bitcast.86, f32[256,256]{1,0:T(8,128)S(1)} %fusion.37, pred[256,256]{1,0:T(8,128)(4,1)S(1)} %fusion.35, f32[256,6,64]{0,2,1:T(8,128)S(1)} %bitcast.76, f32[256,6]{0,1:T(8,128)S(1)} %get-tuple-element.76), kind=kOutput, calls=%fused_computation.7 | convolution fusion | flops 303267840 | bytes 1126400 | tf_op jit(solution)/shard_map/hts,shp->thp/dot_general | solution.py:75
  100.4 3.6 %collective-permute-done.7 = f32[6,65,256]{2,1,0:T(8,128)S(1)} collective-permute-done((f32[6,65,256]{2,1,0:T(8,128)S(1)}, f32[6,65,256]{2,1,0:T(8,128)S(1)}, u32[]{:S(2)}, u32[]{:S(2)}) %collective-permute-start.7) | collective-permute-done | bytes 399392 | tf_op jit(solution)/shard_map/ppermute | solution.py:12
  104.0 1.3 fusion.9
  105.3 1.2 copy.42
  107.3 33.2 %all_to_all.10 = bf16[8,32,384]{2,1,0:T(8,128)(2,1)S(1)} all-to-all(bf16[8,32,384]{2,1,0:T(8,128)(2,1)S(1)} %broadcast_select_fusion), channel_id=1, replica_groups=mesh['seq'=8,'fsdp'=4] {'seq'}, dimensions={0} | all-to-all | bytes 393216 | tf_op jit(solution)/shard_map/all_to_all | solution.py:176
  (81 shorter events, 8.9 us)
Async XLA Ops:
  6.5 47.2 %copy-start = (bf16[2048,384]{1,0:T(8,128)(2,1)S(1)}, bf16[2048,384]{1,0:T(8,128)(2,1)}, u32[]{:S(2)}) copy-start(bf16[2048,384]{1,0:T(8,128)(2,1)} %param.23) | copy-start | bytes 4718596
  6.5 17.1 %copy-start.7 = (s32[4]{0:T(128)S(1)}, s32[4]{0:T(128)}, u32[]{:S(2)}) copy-start(s32[4]{0:T(128)} %param.22) | copy-start | bytes 52
  6.5 17.3 %copy-start.4 = (f32[4,512]{1,0:T(4,128)S(1)}, f32[4,512]{1,0:T(4,128)}, u32[]{:S(2)}) copy-start(f32[4,512]{1,0:T(4,128)} %param.28) | copy-start | bytes 24580
  6.5 37.6 %copy-start.8 = (f32[6]{0:T(128)S(1)}, f32[6]{0:T(128)}, u32[]{:S(2)}) copy-start(f32[6]{0:T(128)} %param.30) | copy-start | bytes 76
  6.5 16.3 %all-to-all-start = ((bf16[8,32,512]{2,1,0:T(8,128)(2,1)}), bf16[8,32,512]{2,1,0:T(8,128)(2,1)S(1)}, u32[]{:S(2)}, u32[]{:S(2)}) async-start(bf16[8,32,512]{2,1,0:T(8,128)(2,1)} %bitcast.81), calls=%async_computation | async-start | bytes 524288 | tf_op jit(solution)/shard_map/all_to_all | solution.py:124
  14.0 41.8 %all-gather.2.cloned.1.call-start = ((), (), s32[]{:S(2)}) async-start(), calls=%async_computation.2 | async-start | bytes 2621440 | tf_op jit(solution)/shard_map/all_gather | solution.py:132
  23.6 9.4 %collective-permute-start = (bf16[256,512]{1,0:T(8,128)(2,1)S(1)}, bf16[256,512]{1,0:T(8,128)(2,1)S(1)}, u32[]{:S(2)}, u32[]{:S(2)}) collective-permute-start(bf16[256,512]{1,0:T(8,128)(2,1)S(1)} %bitcast_select_fusion), channel_id=1, source_target_pairs={{0,1},{1,2},{2,3},{3,0},{4,5},{5,6},{6,7},{7,4},{8,9},{9,10},{10,1... | collective-permute-start | bytes 786440 | tf_op jit(solution)/shard_map/ppermute | solution.py:111
  33.0 10.5 %collective-permute-start.1 = (bf16[256,512]{1,0:T(8,128)(2,1)S(1)}, bf16[256,512]{1,0:T(8,128)(2,1)S(1)}, u32[]{:S(2)}, u32[]{:S(2)}) collective-permute-start(bf16[256,512]{1,0:T(8,128)(2,1)S(1)} %collective-permute-done), channel_id=1, source_target_pairs={{0,1},{1,2},{2,3},{3,0},{4,5},{5,6},{6,7},{7,4},{8,9},{9,10},{10,1... | collective-permute-start | bytes 786440 | tf_op jit(solution)/shard_map/ppermute | solution.py:111
  43.5 5.8 %collective-permute-start.2 = (bf16[256,512]{1,0:T(8,128)(2,1)S(1)}, bf16[256,512]{1,0:T(8,128)(2,1)S(1)}, u32[]{:S(2)}, u32[]{:S(2)}) collective-permute-start(bf16[256,512]{1,0:T(8,128)(2,1)S(1)} %collective-permute-done.1), channel_id=1, source_target_pairs={{0,1},{1,2},{2,3},{3,0},{4,5},{5,6},{6,7},{7,4},{8,9},{9,10},{10,1... | collective-permute-start | bytes 786440 | tf_op jit(solution)/shard_map/ppermute | solution.py:111
  44.1 6.8 %copy-start.3 = (bf16[2048,6]{0,1:T(8,128)(2,1)S(1)}, bf16[2048,6]{0,1:T(8,128)(2,1)}, u32[]{:S(2)}) copy-start(bf16[2048,6]{0,1:T(8,128)(2,1)} %param.26) | copy-start | bytes 73732
  44.1 6.7 %copy-start.5 = (f32[6]{0:T(128)S(1)}, f32[6]{0:T(128)}, u32[]{:S(2)}) copy-start(f32[6]{0:T(128)} %param.29) | copy-start | bytes 76
  49.5 1.4 copy-start.1
  58.4 4.7 %collective-permute-start.3 = (bf16[3,896]{1,0:T(4,128)(2,1)S(1)}, bf16[3,896]{1,0:T(4,128)(2,1)S(1)}, u32[]{:S(2)}, u32[]{:S(2)}) collective-permute-start(bf16[3,896]{1,0:T(4,128)(2,1)S(1)} %pad_maximum_fusion.3), channel_id=1, source_target_pairs={{0,4},{4,8},{8,12},{12,16},{16,20},{20,24},{24,28},{1,5},{5,9},{9,... | collective-permute-start | bytes 16136 | tf_op jit(solution)/shard_map/ppermute | solution.py:12
  64.7 11.7 %collective-permute-start.4 = (f32[6,65,256]{2,1,0:T(8,128)S(1)}, f32[6,65,256]{2,1,0:T(8,128)}, u32[]{:S(2)}, u32[]{:S(2)}) collective-permute-start(f32[6,65,256]{2,1,0:T(8,128)S(1)} %pad_maximum_fusion), channel_id=1, source_target_pairs={{0,4},{4,8},{8,12},{12,16},{16,20},{20,24},{24,28},{1,5},{5,9},{9,... | collective-permute-start | bytes 1198088 | tf_op jit(solution)/shard_map/ppermute | solution.py:12
  69.6 9.3 %collective-permute-start.5 = (f32[6,65,256]{2,1,0:T(8,128)S(1)}, f32[6,65,256]{2,1,0:T(8,128)}, u32[]{:S(2)}, u32[]{:S(2)}) collective-permute-start(f32[6,65,256]{2,1,0:T(8,128)S(1)} %pad_maximum_fusion), channel_id=1, source_target_pairs={{0,8},{4,12},{8,16},{12,20},{16,24},{20,28},{1,9},{5,13},{9,17},{1... | collective-permute-start | bytes 1198088 | tf_op jit(solution)/shard_map/ppermute | solution.py:12
  72.1 16.1 %copy-start.2 = (bf16[256,4096]{1,0:T(8,128)(2,1)S(1)}, bf16[256,4096]{1,0:T(8,128)(2,1)}, u32[]{:S(2)}) copy-start(bf16[256,4096]{1,0:T(8,128)(2,1)} %copy-done.1) | copy-start | bytes 6291460
  81.0 12.3 %collective-permute-start.6 = (f32[6,65,256]{2,1,0:T(8,128)S(1)}, f32[6,65,256]{2,1,0:T(8,128)S(1)}, u32[]{:S(2)}, u32[]{:S(2)}) collective-permute-start(f32[6,65,256]{2,1,0:T(8,128)S(1)} %pad_maximum_fusion.1), channel_id=1, source_target_pairs={{0,8},{4,12},{8,16},{12,20},{16,24},{20,28},{1,9},{5,13},{9,17},{1... | collective-permute-start | bytes 1198088 | tf_op jit(solution)/shard_map/ppermute | solution.py:12
  93.3 10.7 %copy-start.6 = (f32[6]{0:T(128)S(1)}, f32[6]{0:T(128)}, u32[]{:S(2)}) copy-start(f32[6]{0:T(128)} %param.31) | copy-start | bytes 76
  93.4 10.6 %collective-permute-start.7 = (f32[6,65,256]{2,1,0:T(8,128)S(1)}, f32[6,65,256]{2,1,0:T(8,128)S(1)}, u32[]{:S(2)}, u32[]{:S(2)}) collective-permute-start(f32[6,65,256]{2,1,0:T(8,128)S(1)} %pad_maximum_fusion.2), channel_id=1, source_target_pairs={{0,16},{4,20},{8,24},{12,28},{1,17},{5,21},{9,25},{13,29},{2,18},{... | collective-permute-start | bytes 1198088 | tf_op jit(solution)/shard_map/ppermute | solution.py:12
Sparse Core Ops, SparseCore 0:
  16.4 28.1 all-gather.1
